TPU v7x, 512 devices: a whole 4x8x8 slice. The times are simulated.
512 devices in a mesh: call: 8 (over z), tm: 64 (over x, y, core).
Axes of the slice: x: 4, y: 8, z: 8, core: 2. Of those that a mesh axis runs over, the one named last changes fastest.
Arguments:
- frames: bfloat16 [8, 8192, 1024], P('call', 'tm'), may hold values from -6 to 6
- lengths: int32 [8], replicated, may hold values from 2048 to 8192, as said below
- ln_attn_gain: float32 [1024], replicated, may hold values from 0.5 to 1.5
- w_qkv: bfloat16 [1024, 3072], P('tm'), may hold values from -0.1875 to 0.1875
- w_out: bfloat16 [1024, 1024], P('tm'), may hold values from -1.5 to 1.5
- ln_conv_gain: float32 [1024], replicated, may hold values from 0.5 to 1.5
- w_pw1: bfloat16 [1024, 2048], P('tm'), may hold values from -0.1875 to 0.1875
- dw_kernel: float32 [9, 1024], replicated, may hold values from -2 to 2
- bn_gain: float32 [1024], replicated, may hold values from 0.5 to 1.5
- bn_bias: float32 [1024], replicated, may hold values from -3 to 3
Outputs:
- attended: bfloat16 [8, 8192, 1024], P('call', 'tm')
- conv_act: bfloat16 [8, 8192, 1024], P('call', 'tm')
Inputs may be any that keep to these rules, and one draw needn't show every extreme that they name: `lengths`: valid frames of each call; at least one call of the batch fills all 8192 frames.
All inputs are finite; a program needn't handle non-finite values.
Results may differ from a plain program's by a relative error of at most 0.009.
Values may be sent and summed in bfloat16 or wider, within the bound.
No kernel may reach another device: no remote copies, remote signals or barrier semaphores. Data moves between devices by JAX's collectives and lax.ppermute only.
A program may use at most 64 MiB of HBM per device.

v0:
```python
import jax
import jax.numpy as jnp
import numpy as np
from jax import lax
from jax.sharding import Mesh
from jax.sharding import PartitionSpec as P

HEAD_DIM = 64
SPAN = 128
LEFT = 1024
KERNEL = 9
TM = ("x", "y", "core")


def passed_along(value, axis, steps):
    count = lax.axis_size(axis)
    first, last = (max(0, -steps), min(count, count - steps))
    return lax.ppermute(value, axis, [(source, source + steps) for source in range(first, last)])


def with_halo(cells, axis, width):
    count = lax.axis_size(axis)
    ends = count - 1
    head = lax.slice_in_dim(cells, 0, width, axis=0)
    tail = lax.slice_in_dim(cells, cells.shape[0] - width, cells.shape[0], axis=0)
    return jnp.concatenate(
        [
            lax.ppermute(tail, axis, [(i, (i + 1) % count) for i in range(ends)]),
            cells,
            lax.ppermute(head, axis, [((i + 1) % count, i) for i in range(ends)]),
        ],
        axis=0,
    )


def layer_norm(values, gain_vec):
    wide = values.astype(jnp.float32)
    center = wide - jnp.mean(wide, axis=-1, keepdims=True)
    spread = jnp.mean(center * center, axis=-1, keepdims=True)
    return center * lax.rsqrt(spread + 1e-05) * gain_vec


def contract_with(left, rows_piece):
    return jnp.dot(left, rows_piece, preferred_element_type=jnp.float32)


def on_device(
    frames, lengths, ln_attn_gain, w_qkv, w_out, ln_conv_gain, w_pw1, dw_kernel, bn_gain, bn_bias
):
    stream = frames[0]
    frame_count, model_width = stream.shape
    head_count = model_width // HEAD_DIM
    length = lax.dynamic_index_in_dim(lengths, lax.axis_index("call"), 0, keepdims=False)
    first_row = lax.axis_index(TM) * frame_count
    query_pos = first_row + jnp.arange(frame_count, dtype=jnp.int32)
    frame_valid = query_pos < length
    qkv_cols = w_qkv.shape[1]
    out_cols = w_out.shape[1]
    core = lax.axis_index("core")
    cores = lax.axis_size("core")
    swap = [(0, 1), (1, 0)]
    packed = jnp.concatenate([w_qkv, w_out, w_pw1], axis=1)
    half = packed.shape[1] // 2
    halves = (packed[:, :half], packed[:, half:])
    given = lax.ppermute(jnp.where(core == 0, halves[1], halves[0]), "core", swap)
    kept = jnp.where(core == 0, halves[0], halves[1])
    pair = jnp.where(core == 0, jnp.stack([kept, given]), jnp.stack([given, kept]))
    gathered = lax.all_gather(pair.reshape(-1, half), ("x", "y"), axis=0, tiled=True)
    prior_blocks = LEFT // frame_count
    chip_hops = prior_blocks // cores
    blocks = [stream]
    current = stream
    for hop_index in range(chip_hops):
        current = passed_along(current, ("x", "y"), 1)
        blocks.append(current)
    mine = jnp.stack(blocks[::-1])
    gathered, mine = lax.optimization_barrier((gathered, mine))
    other = lax.ppermute(gathered, "core", swap)
    weights = jnp.where(
        core == 0,
        jnp.concatenate([gathered, other], axis=1),
        jnp.concatenate([other, gathered], axis=1),
    )
    theirs = lax.ppermute(mine, "core", swap)
    by_chip = jnp.where(core == 0, jnp.stack([mine, theirs], 1), jnp.stack([theirs, mine], 1))
    by_chip = by_chip.reshape(-1, model_width)
    context_frames = lax.dynamic_slice_in_dim(
        by_chip, core * frame_count, (prior_blocks + 1) * frame_count, 0
    )
    key_count = context_frames.shape[0]
    normed_all = layer_norm(context_frames, ln_attn_gain).astype(jnp.bfloat16)
    normed = normed_all[key_count - frame_count :]
    queries = contract_with(normed, weights[:, :model_width]).astype(jnp.bfloat16)
    key_value = contract_with(normed_all, weights[:, model_width:qkv_cols])
    keys = key_value[:, :model_width].astype(jnp.bfloat16)
    values = key_value[:, model_width:].astype(jnp.bfloat16)
    key_pos = first_row - prior_blocks * frame_count + jnp.arange(key_count, dtype=jnp.int32)
    span_first = query_pos // SPAN * SPAN
    allowed = (key_pos[None, :] >= 0) & (key_pos[None, :] >= span_first[:, None] - LEFT)
    allowed = allowed & (key_pos[None, :] < span_first[:, None] + SPAN)
    allowed = allowed & ((key_pos[None, :] < length) | (key_pos[None, :] == query_pos[:, None]))
    group_size = 4
    group_count = head_count // group_size
    query_groups = queries.reshape(frame_count, group_count, group_size, HEAD_DIM).transpose(
        1, 0, 2, 3
    )
    key_groups = keys.reshape(key_count, group_count, group_size, HEAD_DIM).transpose(1, 0, 2, 3)
    value_groups = values.reshape(key_count, group_count, group_size, HEAD_DIM).transpose(
        1, 0, 2, 3
    )
    scale_factor = 1.0 / jnp.sqrt(jnp.float32(HEAD_DIM))

    def attend_group(operands):
        query_part, key_part, value_part = operands
        scores = (
            jnp.einsum("qhd,khd->hqk", query_part, key_part, preferred_element_type=jnp.float32)
            * scale_factor
        )
        raised = jnp.where(allowed[None], jnp.exp(scores), 0.0)
        probs = (raised / jnp.sum(raised, axis=-1, keepdims=True)).astype(jnp.bfloat16)
        mixed = jnp.einsum("hqk,khd->qhd", probs, value_part, preferred_element_type=jnp.float32)
        return mixed.astype(jnp.bfloat16)

    context = lax.map(attend_group, (query_groups, key_groups, value_groups))
    context = context.transpose(1, 0, 2, 3).reshape(frame_count, model_width)
    projected = contract_with(context, weights[:, qkv_cols : qkv_cols + out_cols])
    attended = jnp.where(frame_valid[:, None], stream.astype(jnp.float32) + projected, 0.0).astype(
        jnp.bfloat16
    )
    conv_in = layer_norm(attended, ln_conv_gain).astype(jnp.bfloat16)
    expanded = contract_with(conv_in, weights[:, qkv_cols + out_cols :])
    gated = expanded[:, :model_width] * jax.nn.sigmoid(expanded[:, model_width:])
    gated = jnp.where(frame_valid[:, None], gated, 0.0).astype(jnp.bfloat16)
    padded = with_halo(gated, TM, KERNEL // 2)
    depthwise = jnp.zeros((frame_count, model_width), jnp.float32)
    for tap_index in range(KERNEL):
        depthwise = (
            depthwise
            + padded[tap_index : tap_index + frame_count].astype(jnp.float32) * dw_kernel[tap_index]
        )
    masked = jnp.where(frame_valid[:, None], depthwise, 0.0)
    moments = (jnp.sum(masked, axis=0), jnp.sum(masked * depthwise, axis=0))
    for axis in ("core", "y", "x", "call"):
        moments = lax.psum(moments, axis)
    first_moment, second_moment = moments
    count_all = jnp.sum(lengths).astype(jnp.float32)
    average = first_moment / count_all
    second = second_moment / count_all
    normal_act = (depthwise - average) * lax.rsqrt(
        second - average * average + 1e-05
    ) * bn_gain + bn_bias
    activated = normal_act * jax.nn.sigmoid(normal_act)
    conv_act = jnp.where(frame_valid[:, None], activated, 0.0).astype(jnp.bfloat16)
    return (attended[None], conv_act[None])


def physical_mesh(mesh):
    devices = mesh.devices
    calls, tms = devices.shape
    first = devices[0]
    xs = len({d.coords[0] for d in first})
    ys = len({d.coords[1] for d in first})
    cores = tms // (xs * ys)
    grid = np.array([[(d.coords[0], d.coords[1], d.core_on_chip) for d in row] for row in devices])
    expect = np.stack(
        np.meshgrid(np.arange(xs), np.arange(ys), np.arange(cores), indexing="ij"), -1
    ).reshape(-1, 3)
    grid = grid - grid[:, :1]
    assert (grid == expect[None]).all()
    return Mesh(devices.reshape(calls, xs, ys, cores), ("call",) + TM)


def solution(mesh):
    mesh4 = physical_mesh(mesh)
    rows = P(TM, None)
    stream = P("call", TM, None)
    return jax.shard_map(
        on_device,
        mesh=mesh4,
        in_specs=(stream, P(), P(), rows, rows, P(), rows, P(), P(), P()),
        out_specs=(stream, stream),
        check_vma=False,
    )
```

profile of v0, /device:TPU:2, one launch (start us, length us, event | category | flops | bytes accessed | tf_op | source)
XLA Modules:
  0.0 247.2 jit_solution(3414614098629872642)
XLA Ops:
  7.2 0.8 constant_dynamic-update-slice_fusion.1
  8.0 0.8 constant_dynamic-update-slice_fusion
  8.9 0.9 select_bitcast_fusion
  9.8 1.9 collective-permute-start
  11.7 1.3 collective-permute-done
  13.0 0.7 maximum_select_fusion.2
  13.7 3.5 %collective-permute-start.1 = (bf16[128,1024]{1,0:T(8,128)(2,1)}, bf16[128,1024]{1,0:T(8,128)(2,1)S(1)}, u32[]{:S(2)}, u32[]{:S(2)}) collective-permute-start(bf16[128,1024]{1,0:T(8,128)(2,1)} %bitcast.81), channel_id=1, source_target_pairs={{0,2},{2,4},{4,6},{6,8},{8,10},{10,12},{12,14},{14,16},{16,18},{18... | collective-permute-start | bytes 786440 | tf_op jit(solution)/shard_map/ppermute | solution.py:18
  17.2 9.1 %collective-permute-done.1 = bf16[128,1024]{1,0:T(8,128)(2,1)S(1)} collective-permute-done((bf16[128,1024]{1,0:T(8,128)(2,1)}, bf16[128,1024]{1,0:T(8,128)(2,1)S(1)}, u32[]{:S(2)}, u32[]{:S(2)}) %collective-permute-start.1) | collective-permute-done | bytes 262176 | tf_op jit(solution)/shard_map/ppermute | solution.py:18
  26.3 1.9 collective-permute-start.2
  28.2 9.7 %collective-permute-done.2 = bf16[128,1024]{1,0:T(8,128)(2,1)S(1)} collective-permute-done((bf16[128,1024]{1,0:T(8,128)(2,1)S(1)}, bf16[128,1024]{1,0:T(8,128)(2,1)S(1)}, u32[]{:S(2)}, u32[]{:S(2)}) %collective-permute-start.2) | collective-permute-done | bytes 262176 | tf_op jit(solution)/shard_map/ppermute | solution.py:18
  37.9 1.9 collective-permute-start.3
  39.8 11.6 %collective-permute-done.3 = bf16[128,1024]{1,0:T(8,128)(2,1)S(1)} collective-permute-done((bf16[128,1024]{1,0:T(8,128)(2,1)S(1)}, bf16[128,1024]{1,0:T(8,128)(2,1)S(1)}, u32[]{:S(2)}, u32[]{:S(2)}) %collective-permute-start.3) | collective-permute-done | bytes 262176 | tf_op jit(solution)/shard_map/ppermute | solution.py:18
  51.4 1.9 collective-permute-start.4
  53.3 9.2 %collective-permute-done.4 = bf16[128,1024]{1,0:T(8,128)(2,1)S(1)} collective-permute-done((bf16[128,1024]{1,0:T(8,128)(2,1)S(1)}, bf16[128,1024]{1,0:T(8,128)(2,1)S(1)}, u32[]{:S(2)}, u32[]{:S(2)}) %collective-permute-start.4) | collective-permute-done | bytes 262176 | tf_op jit(solution)/shard_map/ppermute | solution.py:18
  62.6 48.2 %all-gather.2.cloned.1.call-done = bf16[1024,3072]{1,0:T(8,128)(2,1)} async-done(((bf16[32,3072]{1,0:T(8,128)(2,1)}), bf16[1024,3072]{1,0:T(8,128)(2,1)}) %all-gather.2.cloned.1.call-update) | async-done | bytes 6291472 | tf_op jit(solution)/shard_map/all_gather | solution.py:68
  110.9 1.9 collective-permute-start.6
  112.8 2.4 collective-permute-start.5
  115.8 0.7 broadcast_compare_fusion
  116.5 0.7 fusion.66
  117.2 7.8 %collective-permute-done.5 = bf16[5,128,1024]{2,1,0:T(8,128)(2,1)S(1)} collective-permute-done((bf16[5,128,1024]{2,1,0:T(8,128)(2,1)S(1)}, bf16[5,128,1024]{2,1,0:T(8,128)(2,1)S(1)}, u32[]{:S(2)}, u32[]{:S(2)}) %collective-permute-start.5) | collective-permute-done | bytes 1310752 | tf_op jit(solution)/shard_map/ppermute | solution.py:84
  126.1 0.8 fusion.20
  126.9 0.8 fusion.22
  127.7 0.7 slice-done.1
  128.4 10.2 %maximum_select_fusion = bf16[1024,6144]{1,0:T(8,128)(2,1)S(1)} fusion(bf16[1024,3072]{1,0:T(8,128)(2,1)} %collective-permute-done.6, bf16[1024,3072]{1,0:T(8,128)(2,1)S(1)} %bitcast.75, pred[]{:T(512)S(6)} %eq.6), kind=kLoop, calls=%fused_computation.20 | loop fusion | flops 56623104 | bytes 25165824 | tf_op jit(solution)/shard_map/jit(_where)/select_n | solution.py:79
  139.0 4.1 %copy-done = bf16[1024,6144]{1,0:T(8,128)(2,1)} copy-done((bf16[1024,6144]{1,0:T(8,128)(2,1)}, bf16[1024,6144]{1,0:T(8,128)(2,1)S(1)}, u32[]{:S(2)}) %copy-start) | copy-done | bytes 12582936
  143.1 6.7 %convolution_convert_fusion = bf16[1152,2048]{1,0:T(8,128)(2,1)} fusion(bf16[1152,1024]{1,0:T(8,128)(2,1)S(1)} %fusion.22, bf16[1024,6144]{1,0:T(8,128)(2,1)S(1)} %maximum_select_fusion), kind=kOutput, calls=%fused_computation.21 | convolution fusion | flops 4834197504 | bytes 11272192 | tf_op jit(solution)/shard_map/dot_general | solution.py:44
  150.0 4.3 %fusion.69 = (bf16[1152,1024]{1,0:T(8,128)(2,1)S(1)}, bf16[1152,1024]{1,0:T(8,128)(2,1)}) fusion(bf16[1152,2048]{1,0:T(8,128)(2,1)} %convolution_convert_fusion), kind=kLoop, calls=%fused_computation.109 | loop fusion | bytes 9437184 | tf_op jit(solution)/shard_map/slice | solution.py:95
  154.3 4.3 %copy.16 = bf16[1152,1024]{0,1:T(8,128)(2,1)} copy(bf16[1152,1024]{1,0:T(8,128)(2,1)} %get-tuple-element.103) | data formatting | bytes 4718592 | tf_op jit(solution)/shard_map/slice | solution.py:96
  158.6 2.6 %copy.18 = bf16[1152,1024]{0,1:T(8,128)(2,1)} copy(bf16[1152,1024]{1,0:T(8,128)(2,1)S(1)} %get-tuple-element.102) | data formatting | bytes 4718592 | tf_op jit(solution)/shard_map/slice | solution.py:95
  161.2 15.3 %while.11 = (s32[]{:T(128)}, bf16[4,128,4,64]{1,3,2,0:T(8,128)(2,1)S(1)}, bf16[4,1152,4,64]{1,3,2,0:T(8,128)(2,1)}, bf16[4,128,4,64]{1,3,2,0:T(8,128)(2,1)S(1)},...) while((s32[]{:T(128)}, ...), condition=%wide.region_4.5_spmd.clone, body=%wide.region_2.4_spmd.clone.sunk | while | flops 154420864 | bytes 8694133 | solution.py:124
  161.5 1.7 fusion.85
  163.2 1.8 fusion.86
  165.3 1.7 fusion.85
  167.1 1.8 fusion.86
  169.1 1.7 fusion.85
  170.9 1.7 fusion.86
  172.9 1.7 fusion.85
  174.7 1.8 fusion.86
  176.5 2.2 convert_reduce_fusion.1
  178.9 3.0 %fusion.23 = f32[128,2048]{1,0:T(8,128)S(1)} fusion(bf16[1024,6144]{1,0:T(8,128)(2,1)} %copy-done, bf16[128,1024]{1,0:T(8,128)(2,1)S(1)} %get-tuple-element.120, f32[1024]{0:T(1024)S(1)} %copy-done.7, f32[128]{0:T(128)S(1)} %add_rsqrt_fusion.2, f32[128]{0:T(128)S(1)} %broadcast_multiply_fusion.1), kind=kOutput, calls=%fused_computation.29 | convolution fusion | flops 537526272 | bytes 5510144 | tf_op jit(solution)/shard_map/dot_general | solution.py:44
  182.1 2.0 collective-permute-start.7
  184.2 5.6 %collective-permute-start.8 = (bf16[4,1024]{1,0:T(4,128)(2,1)S(1)}, bf16[4,1024]{1,0:T(4,128)(2,1)S(1)}, u32[]{:S(2)}, u32[]{:S(2)}) collective-permute-start(bf16[4,1024]{1,0:T(4,128)(2,1)S(1)} %get-tuple-element.105), channel_id=1, source_target_pairs={{1,0},{2,1},{3,2},{4,3},{5,4},{6,5},{7,6},{8,7},{9,8},{10,9},{11,1... | collective-permute-start | bytes 24584 | tf_op jit(solution)/shard_map/ppermute | solution.py:30
  191.2 0.7 select_reduce_fusion
  191.8 2.5 %all-reduce.3 = (f32[1024]{0:T(1024)S(1)}, f32[1024]{0:T(1024)S(1)}) all-reduce(f32[1024]{0:T(1024)S(1)} %get-tuple-element.70, f32[1024]{0:T(1024)S(1)} %get-tuple-element.69), channel_id=1, replica_groups=mesh['call'=8,'x'=4,'y'=8,'core'=2] {'core'}, use_global_device_ids=true, to_apply=%region_14.15 | all-reduce | flops 2048 | bytes 16384 | tf_op jit(solution)/shard_map/psum | solution.py:144
  194.3 18.0 %all-reduce = (f32[1024]{0:T(1024)S(1)}, f32[1024]{0:T(1024)S(1)}) all-reduce(f32[1024]{0:T(1024)S(1)} %get-tuple-element.99, f32[1024]{0:T(1024)S(1)} %get-tuple-element.100), channel_id=1, replica_groups=mesh['call'=8,'x'=4,'y'=8,'core'=2] {'y'}, use_global_device_ids=true, to_apply=%region_15.16 | all-reduce | flops 2048 | bytes 16384 | tf_op jit(solution)/shard_map/psum | solution.py:144
  212.3 8.7 %all-reduce.2 = (f32[1024]{0:T(1024)S(1)}, f32[1024]{0:T(1024)S(1)}) all-reduce(f32[1024]{0:T(1024)S(1)} %get-tuple-element.93, f32[1024]{0:T(1024)S(1)} %get-tuple-element.94), channel_id=1, replica_groups=mesh['call'=8,'x'=4,'y'=8,'core'=2] {'x'}, use_global_device_ids=true, to_apply=%region_16.17 | all-reduce | flops 2048 | bytes 16384 | tf_op jit(solution)/shard_map/psum | solution.py:144
  221.0 18.4 %all-reduce.1 = (f32[1024]{0:T(1024)S(1)}, f32[1024]{0:T(1024)S(1)}) all-reduce(f32[1024]{0:T(1024)S(1)} %get-tuple-element.97, f32[1024]{0:T(1024)S(1)} %get-tuple-element.98), channel_id=1, replica_groups=mesh['call'=8,'x'=4,'y'=8,'core'=2] {'call'}, use_global_device_ids=true, to_apply=%region_17.18 | all-reduce | flops 2048 | bytes 16384 | tf_op jit(solution)/shard_map/psum | solution.py:144
  239.4 0.9 fusion.65
  (55 shorter events, 4.8 us)
Async XLA Ops:
  7.2 55.4 %copy-start.1 = (bf16[1,128,1024]{2,1,0:T(8,128)(2,1)S(1)}, bf16[1,128,1024]{2,1,0:T(8,128)(2,1)}, u32[]{:S(2)}) copy-start(bf16[1,128,1024]{2,1,0:T(8,128)(2,1)} %param.12) | copy-start | bytes 786436
  7.2 108.0 %copy-start.8 = (s32[8]{0:T(128)S(1)}, s32[8]{0:T(128)}, u32[]{:S(2)}) copy-start(s32[8]{0:T(128)} %param.13) | copy-start | bytes 100
  7.2 103.7 %all-gather.2.cloned.1.call-start = ((), (), s32[]{:S(2)}) async-start(), calls=%async_computation | async-start | bytes 6488064 | tf_op jit(solution)/shard_map/all_gather | solution.py:68
  9.8 3.2 %collective-permute-start = (bf16[16,3072]{1,0:T(8,128)(2,1)S(1)}, bf16[16,3072]{1,0:T(8,128)(2,1)S(1)}, u32[]{:S(2)}, u32[]{:S(2)}) collective-permute-start(bf16[16,3072]{1,0:T(8,128)(2,1)S(1)} %get-tuple-element.107), channel_id=1, source_target_pairs={{0,1},{1,0},{2,3},{3,2},{4,5},{5,4},{6,7},{7,6},{8,9},{9,8},{10,11... | collective-permute-start | bytes 294920 | tf_op jit(solution)/shard_map/ppermute | solution.py:65
  13.7 12.6 %collective-permute-start.1 = (bf16[128,1024]{1,0:T(8,128)(2,1)}, bf16[128,1024]{1,0:T(8,128)(2,1)S(1)}, u32[]{:S(2)}, u32[]{:S(2)}) collective-permute-start(bf16[128,1024]{1,0:T(8,128)(2,1)} %bitcast.81), channel_id=1, source_target_pairs={{0,2},{2,4},{4,6},{6,8},{8,10},{10,12},{12,14},{14,16},{16,18},{18... | collective-permute-start | bytes 786440 | tf_op jit(solution)/shard_map/ppermute | solution.py:18
  26.3 11.6 %collective-permute-start.2 = (bf16[128,1024]{1,0:T(8,128)(2,1)S(1)}, bf16[128,1024]{1,0:T(8,128)(2,1)S(1)}, u32[]{:S(2)}, u32[]{:S(2)}) collective-permute-start(bf16[128,1024]{1,0:T(8,128)(2,1)S(1)} %collective-permute-done.1), channel_id=1, source_target_pairs={{0,2},{2,4},{4,6},{6,8},{8,10},{10,12},{12,14},{14,16},{16,18},{18... | collective-permute-start | bytes 786440 | tf_op jit(solution)/shard_map/ppermute | solution.py:18
  37.9 13.5 %collective-permute-start.3 = (bf16[128,1024]{1,0:T(8,128)(2,1)S(1)}, bf16[128,1024]{1,0:T(8,128)(2,1)S(1)}, u32[]{:S(2)}, u32[]{:S(2)}) collective-permute-start(bf16[128,1024]{1,0:T(8,128)(2,1)S(1)} %collective-permute-done.2), channel_id=1, source_target_pairs={{0,2},{2,4},{4,6},{6,8},{8,10},{10,12},{12,14},{14,16},{16,18},{18... | collective-permute-start | bytes 786440 | tf_op jit(solution)/shard_map/ppermute | solution.py:18
  51.4 11.1 %collective-permute-start.4 = (bf16[128,1024]{1,0:T(8,128)(2,1)S(1)}, bf16[128,1024]{1,0:T(8,128)(2,1)S(1)}, u32[]{:S(2)}, u32[]{:S(2)}) collective-permute-start(bf16[128,1024]{1,0:T(8,128)(2,1)S(1)} %collective-permute-done.3), channel_id=1, source_target_pairs={{0,2},{2,4},{4,6},{6,8},{8,10},{10,12},{12,14},{14,16},{16,18},{18... | collective-permute-start | bytes 786440 | tf_op jit(solution)/shard_map/ppermute | solution.py:18
  110.9 16.8 %collective-permute-start.6 = (bf16[1024,3072]{1,0:T(8,128)(2,1)}, bf16[1024,3072]{1,0:T(8,128)(2,1)}, u32[]{:S(2)}, u32[]{:S(2)}) collective-permute-start(bf16[1024,3072]{1,0:T(8,128)(2,1)} %all-gather.2.cloned.1.call-done), channel_id=1, source_target_pairs={{0,1},{1,0},{2,3},{3,2},{4,5},{5,4},{6,7},{7,6},{8,9},{9,8},{10,11... | collective-permute-start | bytes 18874376 | tf_op jit(solution)/shard_map/ppermute | solution.py:78
  112.8 12.2 %collective-permute-start.5 = (bf16[5,128,1024]{2,1,0:T(8,128)(2,1)S(1)}, bf16[5,128,1024]{2,1,0:T(8,128)(2,1)S(1)}, u32[]{:S(2)}, u32[]{:S(2)}) collective-permute-start(bf16[5,128,1024]{2,1,0:T(8,128)(2,1)S(1)} %constant_dynamic-update-slice_fusion.2), channel_id=1, source_target_pairs={{0,1},{1,0},{2,3},{3,2},{4,5},{5,4},{6,7},{7,6},{8,9},{9,8},{10,11... | collective-permute-start | bytes 3932168 | tf_op jit(solution)/shard_map/ppermute | solution.py:84
  125.4 2.3 slice-start
  125.7 1.2 copy-start.6
  125.7 2.7 %slice-start.1 = ((s8[6291456]{0:T(1024)(128)(4,1)}), s8[2097152]{0:T(1024)(128)(4,1)S(1)}, s32[]{:S(2)}) async-start(s8[6291456]{0:T(1024)(128)(4,1)} %bitcast.74), calls=%async_computation.2 | async-start | bytes 4194304
  138.6 4.6 %copy-start = (bf16[1024,6144]{1,0:T(8,128)(2,1)}, bf16[1024,6144]{1,0:T(8,128)(2,1)S(1)}, u32[]{:S(2)}) copy-start(bf16[1024,6144]{1,0:T(8,128)(2,1)S(1)} %maximum_select_fusion) | copy-start | bytes 37748740
  176.5 2.4 copy-start.7
  178.6 3.3 %copy-start.2 = (bf16[128,1024]{1,0:T(8,128)(2,1)}, bf16[128,1024]{1,0:T(8,128)(2,1)S(1)}, u32[]{:S(2)}) copy-start(bf16[128,1024]{1,0:T(8,128)(2,1)S(1)} %get-tuple-element.120) | copy-start | bytes 786436
  178.9 10.9 %copy-start.3 = (f32[9,1024]{1,0:T(8,128)S(1)}, f32[9,1024]{1,0:T(8,128)}, u32[]{:S(2)}) copy-start(f32[9,1024]{1,0:T(8,128)} %param.19) | copy-start | bytes 110596
  178.9 60.5 %copy-start.4 = (f32[1024]{0:T(1024)S(1)}, f32[1024]{0:T(1024)}, u32[]{:S(2)}) copy-start(f32[1024]{0:T(1024)} %param.21) | copy-start | bytes 12292
  178.9 60.5 %copy-start.5 = (f32[1024]{0:T(1024)S(1)}, f32[1024]{0:T(1024)}, u32[]{:S(2)}) copy-start(f32[1024]{0:T(1024)} %param.20) | copy-start | bytes 12292
  182.1 9.0 %collective-permute-start.7 = (bf16[4,1024]{1,0:T(4,128)(2,1)S(1)}, bf16[4,1024]{1,0:T(4,128)(2,1)S(1)}, u32[]{:S(2)}, u32[]{:S(2)}) collective-permute-start(bf16[4,1024]{1,0:T(4,128)(2,1)S(1)} %get-tuple-element.104), channel_id=1, source_target_pairs={{0,1},{1,2},{2,3},{3,4},{4,5},{5,6},{6,7},{7,8},{8,9},{9,10},{10,1... | collective-permute-start | bytes 24584 | tf_op jit(solution)/shard_map/ppermute | solution.py:28
  184.2 7.0 %collective-permute-start.8 = (bf16[4,1024]{1,0:T(4,128)(2,1)S(1)}, bf16[4,1024]{1,0:T(4,128)(2,1)S(1)}, u32[]{:S(2)}, u32[]{:S(2)}) collective-permute-start(bf16[4,1024]{1,0:T(4,128)(2,1)S(1)} %get-tuple-element.105), channel_id=1, source_target_pairs={{1,0},{2,1},{3,2},{4,3},{5,4},{6,5},{7,6},{8,7},{9,8},{10,9},{11,1... | collective-permute-start | bytes 24584 | tf_op jit(solution)/shard_map/ppermute | solution.py:30
Sparse Core Ops, SparseCore 0:
  13.8 96.9 all-gather.1
where the time goes:
time: 248 us; the launch traced here: 247 us
  waiting for transfers between devices  96.9 us (39%)
  blocking collectives  47.5 us (19%)
  matrix products  26.3 us (11%)
  starting transfers between devices  23.2 us (9%)
  other arithmetic  19.3 us (8%)
  local copies, waits for them, and re-layouts  18.8 us (8%)
  between operations  15.2 us (6%)
    all_gather x1, waiting for transfers between devices, on_device(): lax.all_gather(pair.reshape(-1, half), ('x', 'y'), axis=0, tiled=True)  48.2 us
    psum x4, blocking collectives, on_device(): moments = lax.psum(moments, axis)  47.5 us
    ppermute x4, waiting for transfers between devices, passed_along(): lax.ppermute(value, axis, [(source, source + steps) for source in range(f...  39.6 us
    dot_general x4, matrix products, contract_with(): return jnp.dot(left, rows_piece, preferred_element_type=jnp.float32)  12.3 us
    select_n x1, other arithmetic, on_device(): jnp.where(core == 0, jnp.concatenate([gathered, other], axis=1), jnp.conc...  10.2 us
    ppermute x4, starting transfers between devices, passed_along(): lax.ppermute(value, axis, [(source, source + steps) for source in range(f...  9.21 us
    ppermute x1, waiting for transfers between devices, on_device(): theirs = lax.ppermute(mine, 'core', swap)  7.81 us
    dot_general x4, matrix products, attend_group(): jnp.einsum('hqk,khd->qhd', probs, value_part, preferred_element_type=jnp....  7 us
  transfers between devices with their start and end apart: 10, of which 7 were waited for; matrix products, arithmetic and copies ran while one was open for 2% of the time, Pallas kernels for 0%

commit v1 on v0

--- a/solution.py
+++ b/solution.py
@@ -65,7 +65,10 @@
     given = lax.ppermute(jnp.where(core == 0, halves[1], halves[0]), "core", swap)
     kept = jnp.where(core == 0, halves[0], halves[1])
     pair = jnp.where(core == 0, jnp.stack([kept, given]), jnp.stack([given, kept]))
-    gathered = lax.all_gather(pair.reshape(-1, half), ("x", "y"), axis=0, tiled=True)
+    unit = pair.reshape(-1, half)
+    current_value = jnp.stack([unit for _ in range(jax.lax.axis_size(("x", "y")))], axis=0)
+    v_now = jax.lax.all_to_all(current_value, ("x", "y"), 0, 0)
+    gathered = jnp.concatenate(v_now, 0)
     prior_blocks = LEFT // frame_count
     chip_hops = prior_blocks // cores
     blocks = [stream]

time: 248 us -> 337 us (1.36)
  waiting for transfers between devices: 96.9 us -> 177 us
  between operations: 15.2 us -> 1.75 us
  starting transfers between devices: 23.2 us -> 36.4 us
    ppermute x4, waiting for transfers between devices: 39.6 us -> 168 us  [passed_along(): lax.ppermute(value, axis, [(source, source + steps) for source in range(f...]
    all_gather x1 -> x0, waiting for transfers between devices: 48.2 us -> none  [on_device(): lax.all_gather(pair.reshape(-1, half), ('x', 'y'), axis=0, tiled=True)]
    all_to_all x0 -> x1, starting transfers between devices: none -> 10.5 us  [on_device(): v_now = jax.lax.all_to_all(current_value, ('x', 'y'), 0, 0)]
    select_n x1, other arithmetic: 10.2 us -> 13.9 us  [on_device(): jnp.where(core == 0, jnp.concatenate([gathered, other], axis=1), jnp.conc...]
    another operation x0 -> x1, local copies, waits for them, and re-layouts: none -> 3.44 us  [on_device(): jnp.stack([unit for _ in range(jax.lax.axis_size(('x', 'y')))], axis=0)]
  transfers between devices with their start and end apart: 10 -> 10, of which waited for: 7 -> 6; matrix products, arithmetic and copies ran while one was open for 2% -> 2% of each run, Pallas kernels for 0% -> 0%
where the time goes in v1:
time: 337 us; the launch traced here: 336 us
  waiting for transfers between devices  177 us (53%)
  blocking collectives  50.6 us (15%)
  starting transfers between devices  36.4 us (11%)
  matrix products  26.3 us (8%)
  other arithmetic  22.4 us (7%)
  local copies, waits for them, and re-layouts  21.5 us (6%)
    ppermute x4, waiting for transfers between devices, passed_along(): lax.ppermute(value, axis, [(source, source + steps) for source in range(f...  168 us
    psum x4, blocking collectives, on_device(): moments = lax.psum(moments, axis)  50.6 us
    select_n x1, other arithmetic, on_device(): jnp.where(core == 0, jnp.concatenate([gathered, other], axis=1), jnp.conc...  13.9 us
    dot_general x4, matrix products, contract_with(): return jnp.dot(left, rows_piece, preferred_element_type=jnp.float32)  12.3 us
    ppermute x4, starting transfers between devices, passed_along(): lax.ppermute(value, axis, [(source, source + steps) for source in range(f...  11.9 us
    all_to_all x1, starting transfers between devices, on_device(): v_now = jax.lax.all_to_all(current_value, ('x', 'y'), 0, 0)  10.5 us
    ppermute x1, waiting for transfers between devices, on_device(): theirs = lax.ppermute(mine, 'core', swap)  7.81 us
    dot_general x4, matrix products, attend_group(): jnp.einsum('hqk,khd->qhd', probs, value_part, preferred_element_type=jnp....  7 us
  transfers between devices with their start and end apart: 10, of which 6 were waited for; matrix products, arithmetic and copies ran while one was open for 2% of the time, Pallas kernels for 0%

profile of v1, /device:TPU:2, one launch (start us, length us, event | category | flops | bytes accessed | tf_op | source)
XLA Modules:
  0.0 335.7 jit_solution(2539460636289066436)
XLA Ops:
  0.6 0.8 constant_dynamic-update-slice_fusion.1
  1.4 0.8 constant_dynamic-update-slice_fusion
  2.2 0.9 select_bitcast_fusion
  3.2 1.9 collective-permute-start
  5.1 1.3 collective-permute-done
  6.4 3.4 %stack.50 = bf16[32,32,3072]{2,1,0:T(8,128)(2,1)} broadcast(bf16[32,3072]{1,0:T(8,128)(2,1)S(1)} %bitcast.79), dimensions={1,2} | broadcast | bytes 6488064 | tf_op jit(solution)/shard_map/stack | solution.py:69
  9.8 10.5 %all-to-all-start = ((bf16[32,32,3072]{2,1,0:T(8,128)(2,1)}), bf16[32,32,3072]{2,1,0:T(8,128)(2,1)}, u32[]{:S(2)}, u32[]{:S(2)}) async-start(bf16[32,32,3072]{2,1,0:T(8,128)(2,1)} %stack.50), calls=%async_computation | async-start | bytes 12582912 | tf_op jit(solution)/shard_map/all_to_all | solution.py:70
  20.4 3.4 %collective-permute-start.1 = (bf16[128,1024]{1,0:T(8,128)(2,1)S(1)}, bf16[128,1024]{1,0:T(8,128)(2,1)S(1)}, u32[]{:S(2)}, u32[]{:S(2)}) collective-permute-start(bf16[128,1024]{1,0:T(8,128)(2,1)S(1)} %bitcast.80), channel_id=1, source_target_pairs={{0,2},{2,4},{4,6},{6,8},{8,10},{10,12},{12,14},{14,16},{16,18},{18... | collective-permute-start | bytes 786440 | tf_op jit(solution)/shard_map/ppermute | solution.py:18
  23.8 143.7 %collective-permute-done.1 = bf16[128,1024]{1,0:T(8,128)(2,1)S(1)} collective-permute-done((bf16[128,1024]{1,0:T(8,128)(2,1)S(1)}, bf16[128,1024]{1,0:T(8,128)(2,1)S(1)}, u32[]{:S(2)}, u32[]{:S(2)}) %collective-permute-start.1) | collective-permute-done | bytes 262176 | tf_op jit(solution)/shard_map/ppermute | solution.py:18
  167.5 4.4 %collective-permute-start.2 = (bf16[128,1024]{1,0:T(8,128)(2,1)S(1)}, bf16[128,1024]{1,0:T(8,128)(2,1)S(1)}, u32[]{:S(2)}, u32[]{:S(2)}) collective-permute-start(bf16[128,1024]{1,0:T(8,128)(2,1)S(1)} %collective-permute-done.1), channel_id=1, source_target_pairs={{0,2},{2,4},{4,6},{6,8},{8,10},{10,12},{12,14},{14,16},{16,18},{18... | collective-permute-start | bytes 786440 | tf_op jit(solution)/shard_map/ppermute | solution.py:18
  171.8 7.1 %collective-permute-done.2 = bf16[128,1024]{1,0:T(8,128)(2,1)S(1)} collective-permute-done((bf16[128,1024]{1,0:T(8,128)(2,1)S(1)}, bf16[128,1024]{1,0:T(8,128)(2,1)S(1)}, u32[]{:S(2)}, u32[]{:S(2)}) %collective-permute-start.2) | collective-permute-done | bytes 262176 | tf_op jit(solution)/shard_map/ppermute | solution.py:18
  179.0 2.3 collective-permute-start.3
  181.2 8.4 %collective-permute-done.3 = bf16[128,1024]{1,0:T(8,128)(2,1)S(1)} collective-permute-done((bf16[128,1024]{1,0:T(8,128)(2,1)S(1)}, bf16[128,1024]{1,0:T(8,128)(2,1)S(1)}, u32[]{:S(2)}, u32[]{:S(2)}) %collective-permute-start.3) | collective-permute-done | bytes 262176 | tf_op jit(solution)/shard_map/ppermute | solution.py:18
  189.6 1.9 collective-permute-start.4
  191.5 8.4 %collective-permute-done.4 = bf16[128,1024]{1,0:T(8,128)(2,1)S(1)} collective-permute-done((bf16[128,1024]{1,0:T(8,128)(2,1)S(1)}, bf16[128,1024]{1,0:T(8,128)(2,1)S(1)}, u32[]{:S(2)}, u32[]{:S(2)}) %collective-permute-start.4) | collective-permute-done | bytes 262176 | tf_op jit(solution)/shard_map/ppermute | solution.py:18
  200.1 1.9 collective-permute-start.6
  202.0 2.4 collective-permute-start.5
  205.1 0.7 broadcast_compare_fusion
  205.8 0.7 fusion.66
  206.4 7.8 %collective-permute-done.5 = bf16[5,128,1024]{2,1,0:T(8,128)(2,1)S(1)} collective-permute-done((bf16[5,128,1024]{2,1,0:T(8,128)(2,1)S(1)}, bf16[5,128,1024]{2,1,0:T(8,128)(2,1)S(1)}, u32[]{:S(2)}, u32[]{:S(2)}) %collective-permute-start.5) | collective-permute-done | bytes 1310752 | tf_op jit(solution)/shard_map/ppermute | solution.py:87
  215.3 0.8 fusion.20
  216.1 0.8 fusion.22
  216.9 13.9 %maximum_select_fusion = bf16[1024,6144]{1,0:T(8,128)(2,1)S(1)} fusion(bf16[1024,3072]{1,0:T(8,128)(2,1)} %collective-permute-done.6, bf16[1024,3072]{1,0:T(8,128)(2,1)} %bitcast.5, pred[]{:T(512)S(6)} %eq.6), kind=kLoop, calls=%fused_computation.20 | loop fusion | flops 56623104 | bytes 25165824 | tf_op jit(solution)/shard_map/jit(_where)/select_n | solution.py:82
  231.3 4.1 %copy-done = bf16[1024,6144]{1,0:T(8,128)(2,1)} copy-done((bf16[1024,6144]{1,0:T(8,128)(2,1)}, bf16[1024,6144]{1,0:T(8,128)(2,1)S(1)}, u32[]{:S(2)}) %copy-start) | copy-done | bytes 12582936
  235.4 6.7 %convolution_convert_fusion = bf16[1152,2048]{1,0:T(8,128)(2,1)} fusion(bf16[1152,1024]{1,0:T(8,128)(2,1)S(1)} %fusion.22, bf16[1024,6144]{1,0:T(8,128)(2,1)S(1)} %maximum_select_fusion), kind=kOutput, calls=%fused_computation.21 | convolution fusion | flops 4834197504 | bytes 11272192 | tf_op jit(solution)/shard_map/dot_general | solution.py:44
  242.3 4.3 %fusion.69 = (bf16[1152,1024]{1,0:T(8,128)(2,1)S(1)}, bf16[1152,1024]{1,0:T(8,128)(2,1)}) fusion(bf16[1152,2048]{1,0:T(8,128)(2,1)} %convolution_convert_fusion), kind=kLoop, calls=%fused_computation.109 | loop fusion | bytes 9437184 | tf_op jit(solution)/shard_map/slice | solution.py:98
  246.6 4.3 %copy.16 = bf16[1152,1024]{0,1:T(8,128)(2,1)} copy(bf16[1152,1024]{1,0:T(8,128)(2,1)} %get-tuple-element.103) | data formatting | bytes 4718592 | tf_op jit(solution)/shard_map/slice | solution.py:99
  250.9 2.6 copy.18
  253.5 15.3 %while.11 = (s32[]{:T(128)}, bf16[4,128,4,64]{1,3,2,0:T(8,128)(2,1)S(1)}, bf16[4,1152,4,64]{1,3,2,0:T(8,128)(2,1)}, bf16[4,128,4,64]{1,3,2,0:T(8,128)(2,1)S(1)},...) while((s32[]{:T(128)}, ...), condition=%wide.region_4.5_spmd.clone, body=%wide.region_2.4_spmd.clone.sunk | while | flops 154420864 | bytes 8694133 | solution.py:127
  253.8 1.7 fusion.85
  255.5 1.7 fusion.86
  257.6 1.7 fusion.85
  259.3 1.8 fusion.86
  261.4 1.7 fusion.85
  263.2 1.8 fusion.86
  265.2 1.7 fusion.85
  267.0 1.7 fusion.86
  268.8 2.2 convert_reduce_fusion.1
  271.2 3.0 fusion.23
  274.4 2.0 collective-permute-start.7
  276.5 5.6 %collective-permute-start.8 = (bf16[4,1024]{1,0:T(4,128)(2,1)S(1)}, bf16[4,1024]{1,0:T(4,128)(2,1)S(1)}, u32[]{:S(2)}, u32[]{:S(2)}) collective-permute-start(bf16[4,1024]{1,0:T(4,128)(2,1)S(1)} %get-tuple-element.105), channel_id=1, source_target_pairs={{1,0},{2,1},{3,2},{4,3},{5,4},{6,5},{7,6},{8,7},{9,8},{10,9},{11,1... | collective-permute-start | bytes 24584 | tf_op jit(solution)/shard_map/ppermute | solution.py:30
  282.2 0.6 reduce_sum.77
  283.5 0.7 select_reduce_fusion
  284.2 2.5 all-reduce.3
  286.6 19.4 %all-reduce = (f32[1024]{0:T(1024)S(1)}, f32[1024]{0:T(1024)S(1)}) all-reduce(f32[1024]{0:T(1024)S(1)} %get-tuple-element.99, f32[1024]{0:T(1024)S(1)} %get-tuple-element.100), channel_id=1, replica_groups=mesh['call'=8,'x'=4,'y'=8,'core'=2] {'y'}, use_global_device_ids=true, to_apply=%region_15.16 | all-reduce | flops 2048 | bytes 16384 | tf_op jit(solution)/shard_map/psum | solution.py:147
  306.0 7.3 %all-reduce.2 = (f32[1024]{0:T(1024)S(1)}, f32[1024]{0:T(1024)S(1)}) all-reduce(f32[1024]{0:T(1024)S(1)} %get-tuple-element.93, f32[1024]{0:T(1024)S(1)} %get-tuple-element.94), channel_id=1, replica_groups=mesh['call'=8,'x'=4,'y'=8,'core'=2] {'x'}, use_global_device_ids=true, to_apply=%region_16.17 | all-reduce | flops 2048 | bytes 16384 | tf_op jit(solution)/shard_map/psum | solution.py:147
  313.3 21.4 %all-reduce.1 = (f32[1024]{0:T(1024)S(1)}, f32[1024]{0:T(1024)S(1)}) all-reduce(f32[1024]{0:T(1024)S(1)} %get-tuple-element.97, f32[1024]{0:T(1024)S(1)} %get-tuple-element.98), channel_id=1, replica_groups=mesh['call'=8,'x'=4,'y'=8,'core'=2] {'call'}, use_global_device_ids=true, to_apply=%region_17.18 | all-reduce | flops 2048 | bytes 16384 | tf_op jit(solution)/shard_map/psum | solution.py:147
  334.8 0.9 fusion.65
  (50 shorter events, 4.1 us)
Async XLA Ops:
  3.2 3.2 collective-permute-start
  9.8 10.6 %copy-start.1 = (bf16[1,128,1024]{2,1,0:T(8,128)(2,1)S(1)}, bf16[1,128,1024]{2,1,0:T(8,128)(2,1)}, u32[]{:S(2)}) copy-start(bf16[1,128,1024]{2,1,0:T(8,128)(2,1)} %param.12) | copy-start | bytes 786436
  9.8 190.3 %all-to-all-start = ((bf16[32,32,3072]{2,1,0:T(8,128)(2,1)}), bf16[32,32,3072]{2,1,0:T(8,128)(2,1)}, u32[]{:S(2)}, u32[]{:S(2)}) async-start(bf16[32,32,3072]{2,1,0:T(8,128)(2,1)} %stack.50), calls=%async_computation | async-start | bytes 12582912 | tf_op jit(solution)/shard_map/all_to_all | solution.py:70
  20.4 184.1 %copy-start.8 = (s32[8]{0:T(128)S(1)}, s32[8]{0:T(128)}, u32[]{:S(2)}) copy-start(s32[8]{0:T(128)} %param.13) | copy-start | bytes 100
  20.4 147.1 %collective-permute-start.1 = (bf16[128,1024]{1,0:T(8,128)(2,1)S(1)}, bf16[128,1024]{1,0:T(8,128)(2,1)S(1)}, u32[]{:S(2)}, u32[]{:S(2)}) collective-permute-start(bf16[128,1024]{1,0:T(8,128)(2,1)S(1)} %bitcast.80), channel_id=1, source_target_pairs={{0,2},{2,4},{4,6},{6,8},{8,10},{10,12},{12,14},{14,16},{16,18},{18... | collective-permute-start | bytes 786440 | tf_op jit(solution)/shard_map/ppermute | solution.py:18
  167.5 11.5 %collective-permute-start.2 = (bf16[128,1024]{1,0:T(8,128)(2,1)S(1)}, bf16[128,1024]{1,0:T(8,128)(2,1)S(1)}, u32[]{:S(2)}, u32[]{:S(2)}) collective-permute-start(bf16[128,1024]{1,0:T(8,128)(2,1)S(1)} %collective-permute-done.1), channel_id=1, source_target_pairs={{0,2},{2,4},{4,6},{6,8},{8,10},{10,12},{12,14},{14,16},{16,18},{18... | collective-permute-start | bytes 786440 | tf_op jit(solution)/shard_map/ppermute | solution.py:18
  179.0 10.6 %collective-permute-start.3 = (bf16[128,1024]{1,0:T(8,128)(2,1)S(1)}, bf16[128,1024]{1,0:T(8,128)(2,1)S(1)}, u32[]{:S(2)}, u32[]{:S(2)}) collective-permute-start(bf16[128,1024]{1,0:T(8,128)(2,1)S(1)} %collective-permute-done.2), channel_id=1, source_target_pairs={{0,2},{2,4},{4,6},{6,8},{8,10},{10,12},{12,14},{14,16},{16,18},{18... | collective-permute-start | bytes 786440 | tf_op jit(solution)/shard_map/ppermute | solution.py:18
  189.6 10.4 %collective-permute-start.4 = (bf16[128,1024]{1,0:T(8,128)(2,1)S(1)}, bf16[128,1024]{1,0:T(8,128)(2,1)S(1)}, u32[]{:S(2)}, u32[]{:S(2)}) collective-permute-start(bf16[128,1024]{1,0:T(8,128)(2,1)S(1)} %collective-permute-done.3), channel_id=1, source_target_pairs={{0,2},{2,4},{4,6},{6,8},{8,10},{10,12},{12,14},{14,16},{16,18},{18... | collective-permute-start | bytes 786440 | tf_op jit(solution)/shard_map/ppermute | solution.py:18
  200.1 16.8 %collective-permute-start.6 = (bf16[1024,3072]{1,0:T(8,128)(2,1)}, bf16[1024,3072]{1,0:T(8,128)(2,1)}, u32[]{:S(2)}, u32[]{:S(2)}) collective-permute-start(bf16[1024,3072]{1,0:T(8,128)(2,1)} %bitcast.5), channel_id=1, source_target_pairs={{0,1},{1,0},{2,3},{3,2},{4,5},{5,4},{6,7},{7,6},{8,9},{9,8},{10,11... | collective-permute-start | bytes 18874376 | tf_op jit(solution)/shard_map/ppermute | solution.py:81
  202.0 12.2 %collective-permute-start.5 = (bf16[5,128,1024]{2,1,0:T(8,128)(2,1)S(1)}, bf16[5,128,1024]{2,1,0:T(8,128)(2,1)S(1)}, u32[]{:S(2)}, u32[]{:S(2)}) collective-permute-start(bf16[5,128,1024]{2,1,0:T(8,128)(2,1)S(1)} %constant_dynamic-update-slice_fusion.2), channel_id=1, source_target_pairs={{0,1},{1,0},{2,3},{3,2},{4,5},{5,4},{6,7},{7,6},{8,9},{9,8},{10,11... | collective-permute-start | bytes 3932168 | tf_op jit(solution)/shard_map/ppermute | solution.py:87
  214.9 1.2 copy-start.6
  230.8 4.6 %copy-start = (bf16[1024,6144]{1,0:T(8,128)(2,1)}, bf16[1024,6144]{1,0:T(8,128)(2,1)S(1)}, u32[]{:S(2)}) copy-start(bf16[1024,6144]{1,0:T(8,128)(2,1)S(1)} %maximum_select_fusion) | copy-start | bytes 37748740
  268.8 2.4 copy-start.7
  270.9 3.3 copy-start.2
  271.2 10.9 %copy-start.3 = (f32[9,1024]{1,0:T(8,128)S(1)}, f32[9,1024]{1,0:T(8,128)}, u32[]{:S(2)}) copy-start(f32[9,1024]{1,0:T(8,128)} %param.19) | copy-start | bytes 110596
  271.2 63.6 %copy-start.4 = (f32[1024]{0:T(1024)S(1)}, f32[1024]{0:T(1024)}, u32[]{:S(2)}) copy-start(f32[1024]{0:T(1024)} %param.21) | copy-start | bytes 12292
  271.2 63.6 %copy-start.5 = (f32[1024]{0:T(1024)S(1)}, f32[1024]{0:T(1024)}, u32[]{:S(2)}) copy-start(f32[1024]{0:T(1024)} %param.20) | copy-start | bytes 12292
  274.4 9.0 %collective-permute-start.7 = (bf16[4,1024]{1,0:T(4,128)(2,1)S(1)}, bf16[4,1024]{1,0:T(4,128)(2,1)S(1)}, u32[]{:S(2)}, u32[]{:S(2)}) collective-permute-start(bf16[4,1024]{1,0:T(4,128)(2,1)S(1)} %get-tuple-element.104), channel_id=1, source_target_pairs={{0,1},{1,2},{2,3},{3,4},{4,5},{5,6},{6,7},{7,8},{8,9},{9,10},{10,1... | collective-permute-start | bytes 24584 | tf_op jit(solution)/shard_map/ppermute | solution.py:28
  276.5 7.0 %collective-permute-start.8 = (bf16[4,1024]{1,0:T(4,128)(2,1)S(1)}, bf16[4,1024]{1,0:T(4,128)(2,1)S(1)}, u32[]{:S(2)}, u32[]{:S(2)}) collective-permute-start(bf16[4,1024]{1,0:T(4,128)(2,1)S(1)} %get-tuple-element.105), channel_id=1, source_target_pairs={{1,0},{2,1},{3,2},{4,3},{5,4},{6,5},{7,6},{8,7},{9,8},{10,9},{11,1... | collective-permute-start | bytes 24584 | tf_op jit(solution)/shard_map/ppermute | solution.py:30
